TPU v7x, 32 devices: a whole 2x2x4 slice. The times are simulated.
32 devices in a mesh: section: 2 (over x), dp: 4 (over z), mp: 4 (over y, core).
Axes of the slice: x: 2, y: 2, z: 4, core: 2. Of those that a mesh axis runs over, the one named last changes fastest.
Arguments:
- queries: bfloat16 [2, 4, 640, 4096], P('section', 'dp', None, 'mp')
- keys: bfloat16 [2, 4, 640, 4096], P('section', 'dp', None, 'mp')
- values: bfloat16 [2, 4, 640, 4096], P('section', 'dp', None, 'mp'), may hold values from -6 to 6
- grad_out: bfloat16 [2, 4, 640, 4096], P('section', 'dp', None, 'mp'), may hold values from -6 to 6
- positions: int32 [2, 4, 640], P('section', 'dp'), may hold values from 0 to 319, as said below
Outputs:
- received: bfloat16 [2, 4, 3, 640, 4096], P('section', 'dp', None, 'mp')
- bias_grad: float32 [2, 3, 4096], P('section')
Inputs may be any that keep to these rules, and one draw needn't show every extreme that they name: `positions`: along each sequence a position is 0 or one more than the position before it; the first is 0; a document starts at token 320, and none is longer than 320 tokens.
All inputs are finite; a program needn't handle non-finite values.
Results may differ from a plain program's by a relative error of at most 0.0065.
Values may be sent and summed in bfloat16 or wider, within the bound.
No kernel may reach another device: no remote copies, remote signals or barrier semaphores. Data moves between devices by JAX's collectives and lax.ppermute only.
A program may use at most 64 MiB of HBM per device.

v0:
```python
import math
import jax
import jax.numpy as jnp
from jax import lax
from jax.sharding import PartitionSpec as P

HEAD_DIM = 128
CHUNK_HEADS = 2


def chunk_grads(query_rows, key_rows, value_rows, grad_rows, allowed, halves):
    length, width = query_rows.shape
    heads = width // HEAD_DIM
    block = length // halves
    scaling = 1.0 / math.sqrt(HEAD_DIM)

    def split(rows):
        return rows.reshape(halves, block, heads, HEAD_DIM)

    q, k, v, g = (split(query_rows), split(key_rows), split(value_rows), split(grad_rows))
    scores = jnp.einsum("bqhd,bkhd->bhqk", q, k, preferred_element_type=jnp.float32) * scaling
    scores = jnp.where(allowed[:, None], scores, jnp.float32(-1e30))
    highest = jnp.max(scores, axis=-1, keepdims=True)
    expont = jnp.exp(scores - highest)
    attn = expont / jnp.sum(expont, axis=-1, keepdims=True)
    attn_low = attn.astype(jnp.bfloat16)
    grad_v = jnp.einsum("bhqk,bqhd->bkhd", attn_low, g, preferred_element_type=jnp.float32)
    grad_attn = jnp.einsum("bqhd,bkhd->bhqk", g, v, preferred_element_type=jnp.float32)
    delta = jnp.sum(attn * grad_attn, axis=-1, keepdims=True)
    grad_scores = (attn * (grad_attn - delta) * scaling).astype(jnp.bfloat16)
    grad_q = jnp.einsum("bhqk,bkhd->bqhd", grad_scores, k, preferred_element_type=jnp.float32)
    grad_k = jnp.einsum("bhqk,bqhd->bkhd", grad_scores, q, preferred_element_type=jnp.float32)
    blocks = jnp.stack([grad_q, grad_k, grad_v]).astype(jnp.bfloat16)
    return blocks.reshape(3, length, width)


def per_device(queries, keys, values, grad_out, positions):
    query_rows = queries[0, 0]
    key_rows = keys[0, 0]
    value_rows = values[0, 0]
    grad_rows = grad_out[0, 0]
    token_positions = positions[0, 0]
    length, columns = query_rows.shape
    sections = lax.axis_size("section")
    parts = lax.axis_size("mp")
    replicas = lax.axis_size("dp")
    part = lax.axis_index("mp")
    rows = length // parts
    halves = 2
    block = length // halves
    local = jnp.arange(block, dtype=jnp.int32)
    pos = token_positions.reshape(halves, block)
    allowed = (local[None, None, :] <= local[None, :, None]) & (
        local[None, None, :] >= (local[None, :] - pos)[:, :, None]
    )

    def pairs(shift):
        return [
            ((s + 1) * parts + m, s * parts + (m + shift) % parts)
            for s in range(sections - 1)
            for m in range(parts)
        ]

    width = CHUNK_HEADS * HEAD_DIM
    chunk_count = columns // width
    arrived = [[None] * chunk_count for _ in range(parts)]
    sums = []
    for c in range(chunk_count):
        cols = slice(c * width, (c + 1) * width)
        grads = chunk_grads(
            query_rows[:, cols],
            key_rows[:, cols],
            value_rows[:, cols],
            grad_rows[:, cols],
            allowed,
            halves,
        )
        sums.append(jnp.sum(grads.astype(jnp.float32), axis=1))
        for shift in range(parts):
            target = (part + shift) % parts
            piece = lax.dynamic_slice_in_dim(grads, target * rows, rows, 1)
            arrived[shift][c] = lax.ppermute(piece, ("section", "mp"), pairs(shift))
    own = jnp.concatenate(sums, axis=1)
    slots = lax.dynamic_update_slice_in_dim(
        jnp.zeros((3, columns * parts), jnp.float32), own, part * columns, 1
    )
    totals = lax.psum(slots, ("dp", "mp"))
    totals = lax.ppermute(totals, "section", [(s + 1, s) for s in range(sections - 1)])
    bias_grad = totals / math.sqrt(replicas * length)
    received = jnp.zeros((3, rows, columns * parts), jnp.bfloat16)
    for shift in range(parts):
        source = (part - shift) % parts
        piece = jnp.concatenate(arrived[shift], axis=2)
        received = lax.dynamic_update_slice_in_dim(received, piece, source * columns, 2)
    return (received[None, None], bias_grad[None])


def solution(mesh):
    return jax.shard_map(
        per_device,
        mesh=mesh,
        in_specs=(
            P("section", "dp", None, "mp"),
            P("section", "dp", None, "mp"),
            P("section", "dp", None, "mp"),
            P("section", "dp", None, "mp"),
            P("section", "dp", None),
        ),
        out_specs=(P("section", "dp", None, "mp", None), P("section", None, None)),
        check_vma=False,
    )
```

profile of v0, /device:TPU:5, one launch (start us, length us, event | category | flops | bytes accessed | tf_op | source)
XLA Modules:
  0.0 251.5 jit_solution(15631880437137905530)
XLA Ops:
  0.7 2.3 fusion.237
  5.7 2.2 fusion.239
  10.6 1.5 fusion.135
  12.1 3.2 %fusion.256 = (f32[2,2,320]{2,1,0:T(2,128)S(1)}, f32[2,2,320,320]{2,3,1,0:T(8,128)}) fusion(pred[2,320,320]{1,2,0:T(8,128)(4,1)S(1)} %fusion.124, bf16[2,320,2,128]{3,2,1,0:T(2,128)(2,1)} %reshape.143, bf16[2,320,2,128]{3,2,1,0:T(2,128)(2,1)} %reshape.142), kind=kOutput, calls=%fused_computation.205 | convolution fusion | flops 106496320 | bytes 2503680 | tf_op jit(solution)/shard_map/sub | solution.py:24
  15.3 3.8 %fusion.75 = bf16[2,320,2,128]{3,1,2,0:T(8,128)(2,1)} fusion(f32[2,2,320,320]{2,3,1,0:T(8,128)S(1)} %fusion.135, bf16[2,320,2,128]{3,2,1,0:T(2,128)(2,1)} %reshape.143, f32[2,2,320,320]{2,3,1,0:T(8,128)} %get-tuple-element.41, f32[2,2,320]{2,1,0:T(2,128)S(1)} %get-tuple-element.40), kind=kOutput, calls=%fused_computation.57 | convolution fusion | flops 107890240 | bytes 3937280 | tf_op jit(solution)/shard_map/bhqk,bkhd->bqhd/dot_general | solution.py:31
  19.0 3.6 %fusion.72 = bf16[2,320,2,128]{3,1,2,0:T(8,128)(2,1)} fusion(f32[2,2,320,320]{2,3,1,0:T(8,128)S(1)} %fusion.135, bf16[2,320,2,128]{3,2,1,0:T(2,128)(2,1)} %reshape.142, f32[2,2,320,320]{2,3,1,0:T(8,128)} %get-tuple-element.41, f32[2,2,320]{2,1,0:T(2,128)S(1)} %get-tuple-element.40), kind=kOutput, calls=%fused_computation.56 | convolution fusion | flops 107890240 | bytes 3937280 | tf_op jit(solution)/shard_map/bhqk,bqhd->bkhd/dot_general | solution.py:32
  22.7 2.8 %fusion.96 = bf16[2,320,2,128]{3,1,2,0:T(8,128)(2,1)} fusion(bf16[2,320,2,128]{3,2,1,0:T(2,128)(2,1)} %reshape.144, f32[2,2,320,320]{2,3,1,0:T(8,128)} %get-tuple-element.41, f32[2,2,320]{2,1,0:T(2,128)S(1)} %get-tuple-element.40), kind=kOutput, calls=%fused_computation.64 | convolution fusion | flops 105840640 | bytes 2298880 | tf_op jit(solution)/shard_map/bhqk,bqhd->bkhd/dot_general | solution.py:27
  27.3 2.1 fusion.251
  29.4 1.5 fusion.133
  30.9 3.8 %fusion.81 = bf16[2,320,2,128]{3,1,2,0:T(8,128)(2,1)} fusion(f32[2,2,320,320]{2,3,1,0:T(8,128)S(1)} %fusion.133, bf16[2,320,2,128]{3,2,1,0:T(2,128)(2,1)} %copy-done.22, f32[2,2,320,320]{2,3,1,0:T(8,128)} %get-tuple-element.39, f32[2,2,320]{2,1,0:T(2,128)S(1)} %get-tuple-element.38), kind=kOutput, calls=%fused_computation.59 | convolution fusion | flops 107890240 | bytes 3937280 | tf_op jit(solution)/shard_map/bhqk,bkhd->bqhd/dot_general | solution.py:31
  34.7 3.6 %fusion.78 = bf16[2,320,2,128]{3,1,2,0:T(8,128)(2,1)} fusion(f32[2,2,320,320]{2,3,1,0:T(8,128)S(1)} %fusion.133, bf16[2,320,2,128]{3,2,1,0:T(2,128)(2,1)} %copy-done.20, f32[2,2,320,320]{2,3,1,0:T(8,128)} %get-tuple-element.39, f32[2,2,320]{2,1,0:T(2,128)S(1)} %get-tuple-element.38), kind=kOutput, calls=%fused_computation.58 | convolution fusion | flops 107890240 | bytes 3937280 | tf_op jit(solution)/shard_map/bhqk,bqhd->bkhd/dot_general | solution.py:32
  38.3 2.8 %fusion.97 = bf16[2,320,2,128]{3,1,2,0:T(8,128)(2,1)} fusion(bf16[2,320,2,128]{3,2,1,0:T(2,128)(2,1)} %reshape.148, f32[2,2,320,320]{2,3,1,0:T(8,128)} %get-tuple-element.39, f32[2,2,320]{2,1,0:T(2,128)S(1)} %get-tuple-element.38), kind=kOutput, calls=%fused_computation.65 | convolution fusion | flops 105840640 | bytes 2298880 | tf_op jit(solution)/shard_map/bhqk,bqhd->bkhd/dot_general | solution.py:27
  43.0 2.1 fusion.246
  45.1 1.5 fusion.131
  46.6 3.8 %fusion.87 = bf16[2,320,2,128]{3,1,2,0:T(8,128)(2,1)} fusion(f32[2,2,320,320]{2,3,1,0:T(8,128)S(1)} %fusion.131, bf16[2,320,2,128]{3,2,1,0:T(2,128)(2,1)} %copy-done.23, f32[2,2,320,320]{2,3,1,0:T(8,128)} %get-tuple-element.37, f32[2,2,320]{2,1,0:T(2,128)S(1)} %get-tuple-element.36), kind=kOutput, calls=%fused_computation.61 | convolution fusion | flops 107890240 | bytes 3937280 | tf_op jit(solution)/shard_map/bhqk,bkhd->bqhd/dot_general | solution.py:31
  50.4 3.6 %fusion.84 = bf16[2,320,2,128]{3,1,2,0:T(8,128)(2,1)} fusion(f32[2,2,320,320]{2,3,1,0:T(8,128)S(1)} %fusion.131, bf16[2,320,2,128]{3,2,1,0:T(2,128)(2,1)} %copy-done.21, f32[2,2,320,320]{2,3,1,0:T(8,128)} %get-tuple-element.37, f32[2,2,320]{2,1,0:T(2,128)S(1)} %get-tuple-element.36), kind=kOutput, calls=%fused_computation.60 | convolution fusion | flops 107890240 | bytes 3937280 | tf_op jit(solution)/shard_map/bhqk,bqhd->bkhd/dot_general | solution.py:32
  54.0 2.7 %fusion.98 = bf16[2,320,2,128]{3,1,2,0:T(8,128)(2,1)} fusion(bf16[2,320,2,128]{3,2,1,0:T(2,128)(2,1)} %reshape.152, f32[2,2,320,320]{2,3,1,0:T(8,128)} %get-tuple-element.37, f32[2,2,320]{2,1,0:T(2,128)S(1)} %get-tuple-element.36), kind=kOutput, calls=%fused_computation.66 | convolution fusion | flops 105840640 | bytes 2298880 | tf_op jit(solution)/shard_map/bhqk,bqhd->bkhd/dot_general | solution.py:27
  57.0 2.3 fusion.241
  59.8 3.6 %fusion.90 = bf16[2,320,2,128]{3,1,2,0:T(8,128)(2,1)} fusion(f32[2,2,320,320]{2,3,1,0:T(8,128)S(1)} %fusion.129, bf16[2,320,2,128]{3,2,1,0:T(2,128)(2,1)S(1)} %reshape.154, f32[2,2,320,320]{2,3,1,0:T(8,128)} %get-tuple-element.35, f32[2,2,320]{2,1,0:T(2,128)S(1)} %get-tuple-element.34), kind=kOutput, calls=%fused_computation.62 | convolution fusion | flops 107890240 | bytes 3937280 | tf_op jit(solution)/shard_map/bhqk,bqhd->bkhd/dot_general | solution.py:32
  63.4 3.7 %fusion.93 = bf16[2,320,2,128]{3,1,2,0:T(8,128)(2,1)} fusion(f32[2,2,320,320]{2,3,1,0:T(8,128)S(1)} %fusion.129, bf16[2,320,2,128]{3,2,1,0:T(2,128)(2,1)S(1)} %reshape.155, f32[2,2,320,320]{2,3,1,0:T(8,128)} %get-tuple-element.35, f32[2,2,320]{2,1,0:T(2,128)S(1)} %get-tuple-element.34), kind=kOutput, calls=%fused_computation.63 | convolution fusion | flops 107890240 | bytes 3937280 | tf_op jit(solution)/shard_map/bhqk,bkhd->bqhd/dot_general | solution.py:31
  67.1 2.7 %fusion.99 = bf16[2,320,2,128]{3,1,2,0:T(8,128)(2,1)} fusion(bf16[2,320,2,128]{3,2,1,0:T(2,128)(2,1)S(1)} %reshape.156, f32[2,2,320,320]{2,3,1,0:T(8,128)} %get-tuple-element.35, f32[2,2,320]{2,1,0:T(2,128)S(1)} %get-tuple-element.34), kind=kOutput, calls=%fused_computation.67 | convolution fusion | flops 105840640 | bytes 2298880 | tf_op jit(solution)/shard_map/bhqk,bqhd->bkhd/dot_general | solution.py:27
  75.5 2.0 copy.41
  78.7 2.0 copy.43
  80.7 1.9 stack.58
  86.1 2.0 copy.50
  88.2 1.9 stack.60
  90.1 1.7 constant_dynamic-update-slice_fusion.11
  91.8 2.0 copy.54
  93.8 1.9 stack.62
  96.4 1.7 constant_dynamic-update-slice_fusion.9
  99.6 53.4 %psum.7 = f32[3,4096]{1,0:T(4,128)} all-reduce(f32[3,4096]{1,0:T(4,128)S(1)} %maximum_dynamic-update-slice_fusion), channel_id=1, replica_groups=mesh['section'=2,'dp'=4,'mp'=4] {'dp','mp'}, use_global_device_ids=true, to_apply=%region_16.17 | all-reduce | flops 12288 | bytes 98304 | tf_op jit(solution)/shard_map/psum | solution.py:87
  155.1 1.4 collective-permute-start
  157.4 1.4 collective-permute-start.1
  165.9 1.5 collective-permute-done.1
  168.7 4.0 %collective-permute-done.2 = bf16[3,160,256]{2,1,0:T(8,128)(2,1)S(1)} collective-permute-done((bf16[3,160,256]{2,1,0:T(8,128)(2,1)}, bf16[3,160,256]{2,1,0:T(8,128)(2,1)S(1)}, u32[]{:S(2)}, u32[]{:S(2)}) %collective-permute-start.2) | collective-permute-done | bytes 245792 | tf_op jit(solution)/shard_map/ppermute | solution.py:82
  174.0 3.9 %collective-permute-done.3 = bf16[3,160,256]{2,1,0:T(8,128)(2,1)S(1)} collective-permute-done((bf16[3,160,256]{2,1,0:T(8,128)(2,1)}, bf16[3,160,256]{2,1,0:T(8,128)(2,1)S(1)}, u32[]{:S(2)}, u32[]{:S(2)}) %collective-permute-start.3) | collective-permute-done | bytes 245792 | tf_op jit(solution)/shard_map/ppermute | solution.py:82
  179.1 12.5 %collective-permute-done.4 = bf16[3,160,256]{2,1,0:T(8,128)(2,1)S(1)} collective-permute-done((bf16[3,160,256]{2,1,0:T(8,128)(2,1)}, bf16[3,160,256]{2,1,0:T(8,128)(2,1)S(1)}, u32[]{:S(2)}, u32[]{:S(2)}) %collective-permute-start.4) | collective-permute-done | bytes 245792 | tf_op jit(solution)/shard_map/ppermute | solution.py:82
  193.0 4.0 %collective-permute-done.5 = bf16[3,160,256]{2,1,0:T(8,128)(2,1)S(1)} collective-permute-done((bf16[3,160,256]{2,1,0:T(8,128)(2,1)}, bf16[3,160,256]{2,1,0:T(8,128)(2,1)S(1)}, u32[]{:S(2)}, u32[]{:S(2)}) %collective-permute-start.5) | collective-permute-done | bytes 245792 | tf_op jit(solution)/shard_map/ppermute | solution.py:82
  198.9 3.3 %collective-permute-done.6 = bf16[3,160,256]{2,1,0:T(8,128)(2,1)S(1)} collective-permute-done((bf16[3,160,256]{2,1,0:T(8,128)(2,1)S(1)}, bf16[3,160,256]{2,1,0:T(8,128)(2,1)S(1)}, u32[]{:S(2)}, u32[]{:S(2)}) %collective-permute-start.6) | collective-permute-done | bytes 245792 | tf_op jit(solution)/shard_map/ppermute | solution.py:82
  205.1 2.0 collective-permute-done.7
  209.8 4.1 %collective-permute-done.9 = bf16[3,160,256]{2,1,0:T(8,128)(2,1)S(1)} collective-permute-done((bf16[3,160,256]{2,1,0:T(8,128)(2,1)S(1)}, bf16[3,160,256]{2,1,0:T(8,128)(2,1)S(1)}, u32[]{:S(2)}, u32[]{:S(2)}) %collective-permute-start.9) | collective-permute-done | bytes 245792 | tf_op jit(solution)/shard_map/ppermute | solution.py:82
  215.1 4.0 %collective-permute-done.10 = bf16[3,160,256]{2,1,0:T(8,128)(2,1)S(1)} collective-permute-done((bf16[3,160,256]{2,1,0:T(8,128)(2,1)S(1)}, bf16[3,160,256]{2,1,0:T(8,128)(2,1)S(1)}, u32[]{:S(2)}, u32[]{:S(2)}) %collective-permute-start.10) | collective-permute-done | bytes 245792 | tf_op jit(solution)/shard_map/ppermute | solution.py:82
  220.5 3.9 %collective-permute-done.11 = bf16[3,160,256]{2,1,0:T(8,128)(2,1)S(1)} collective-permute-done((bf16[3,160,256]{2,1,0:T(8,128)(2,1)S(1)}, bf16[3,160,256]{2,1,0:T(8,128)(2,1)S(1)}, u32[]{:S(2)}, u32[]{:S(2)}) %collective-permute-start.11) | collective-permute-done | bytes 245792 | tf_op jit(solution)/shard_map/ppermute | solution.py:82
  224.5 13.4 %collective-permute-done.12 = bf16[3,160,256]{2,1,0:T(8,128)(2,1)S(1)} collective-permute-done((bf16[3,160,256]{2,1,0:T(8,128)(2,1)S(1)}, bf16[3,160,256]{2,1,0:T(8,128)(2,1)S(1)}, u32[]{:S(2)}, u32[]{:S(2)}) %collective-permute-start.12) | collective-permute-done | bytes 245792 | tf_op jit(solution)/shard_map/ppermute | solution.py:82
  237.9 5.3 %collective-permute-done.13 = bf16[3,160,256]{2,1,0:T(8,128)(2,1)S(1)} collective-permute-done((bf16[3,160,256]{2,1,0:T(8,128)(2,1)S(1)}, bf16[3,160,256]{2,1,0:T(8,128)(2,1)S(1)}, u32[]{:S(2)}, u32[]{:S(2)}) %collective-permute-start.13) | collective-permute-done | bytes 245792 | tf_op jit(solution)/shard_map/ppermute | solution.py:82
  243.2 3.6 %collective-permute-done.14 = bf16[3,160,256]{2,1,0:T(8,128)(2,1)S(1)} collective-permute-done((bf16[3,160,256]{2,1,0:T(8,128)(2,1)S(1)}, bf16[3,160,256]{2,1,0:T(8,128)(2,1)S(1)}, u32[]{:S(2)}, u32[]{:S(2)}) %collective-permute-start.14) | collective-permute-done | bytes 245792 | tf_op jit(solution)/shard_map/ppermute | solution.py:82
  246.8 2.6 %collective-permute-done.15 = bf16[3,160,256]{2,1,0:T(8,128)(2,1)S(1)} collective-permute-done((bf16[3,160,256]{2,1,0:T(8,128)(2,1)S(1)}, bf16[3,160,256]{2,1,0:T(8,128)(2,1)S(1)}, u32[]{:S(2)}, u32[]{:S(2)}) %collective-permute-start.15) | collective-permute-done | bytes 245792 | tf_op jit(solution)/shard_map/ppermute | solution.py:82
  249.6 1.9 copy-done.1
  (139 shorter events, 47.4 us)
Async XLA Ops:
  0.6 3.2 %copy-start.10 = (bf16[1,1,640,1024]{3,2,1,0:T(8,128)(2,1)S(1)}, bf16[1,1,640,1024]{3,2,1,0:T(8,128)(2,1)}, u32[]{:S(2)}) copy-start(bf16[1,1,640,1024]{3,2,1,0:T(8,128)(2,1)} %param.6) | copy-start | bytes 3932164
  3.0 2.5 %copy-start.26 = (s32[1,1,640]{2,1,0:T(1,128)S(1)}, s32[1,1,640]{2,1,0:T(1,128)}, u32[]{:S(2)}) copy-start(s32[1,1,640]{2,1,0:T(1,128)} %param.9) | copy-start | bytes 7684
  4.8 3.9 %copy-start.11 = (bf16[1,1,640,1024]{3,2,1,0:T(8,128)(2,1)S(1)}, bf16[1,1,640,1024]{3,2,1,0:T(8,128)(2,1)}, u32[]{:S(2)}) copy-start(bf16[1,1,640,1024]{3,2,1,0:T(8,128)(2,1)} %param.7) | copy-start | bytes 3932164
  22.7 2.8 %copy-start.6 = (bf16[640,256]{1,0:T(8,128)(2,1)S(1)}, bf16[640,256]{1,0:T(8,128)(2,1)}, u32[]{:S(2)}) copy-start(bf16[640,256]{1,0:T(8,128)(2,1)} %get-tuple-element.5) | copy-start | bytes 983044
  22.7 2.9 %copy-start.7 = (bf16[640,256]{1,0:T(8,128)(2,1)S(1)}, bf16[640,256]{1,0:T(8,128)(2,1)}, u32[]{:S(2)}) copy-start(bf16[640,256]{1,0:T(8,128)(2,1)} %get-tuple-element.9) | copy-start | bytes 983044
  22.7 3.0 %copy-start.8 = (bf16[640,256]{1,0:T(8,128)(2,1)S(1)}, bf16[640,256]{1,0:T(8,128)(2,1)}, u32[]{:S(2)}) copy-start(bf16[640,256]{1,0:T(8,128)(2,1)} %get-tuple-element.13) | copy-start | bytes 983044
  25.5 1.0 copy-start.9
  25.5 1.7 copy-start.20
  25.7 1.6 copy-start.22
  38.3 2.8 %copy-start.2 = (bf16[640,256]{1,0:T(8,128)(2,1)S(1)}, bf16[640,256]{1,0:T(8,128)(2,1)}, u32[]{:S(2)}) copy-start(bf16[640,256]{1,0:T(8,128)(2,1)} %get-tuple-element.4) | copy-start | bytes 983044
  38.3 2.9 %copy-start.3 = (bf16[640,256]{1,0:T(8,128)(2,1)S(1)}, bf16[640,256]{1,0:T(8,128)(2,1)}, u32[]{:S(2)}) copy-start(bf16[640,256]{1,0:T(8,128)(2,1)} %get-tuple-element.8) | copy-start | bytes 983044
  38.3 3.0 %copy-start.4 = (bf16[640,256]{1,0:T(8,128)(2,1)S(1)}, bf16[640,256]{1,0:T(8,128)(2,1)}, u32[]{:S(2)}) copy-start(bf16[640,256]{1,0:T(8,128)(2,1)} %get-tuple-element.12) | copy-start | bytes 983044
  41.1 1.0 copy-start.5
  41.2 1.8 copy-start.21
  41.3 1.7 copy-start.23
  67.1 2.7 %copy-start.16 = (bf16[2,320,2,128]{3,1,2,0:T(8,128)(2,1)S(1)}, bf16[2,320,2,128]{3,1,2,0:T(8,128)(2,1)}, u32[]{:S(2)}) copy-start(bf16[2,320,2,128]{3,1,2,0:T(8,128)(2,1)} %fusion.75) | copy-start | bytes 983044
  69.8 1.0 copy-start.13
  69.8 1.5 copy-start.12
  71.4 1.0 copy-start.17
  72.0 1.0 copy-start.15
  72.0 1.5 copy-start.14
  73.9 1.0 copy-start.18
  82.6 1.2 copy-start.19
  152.9 10.2 %collective-permute-start.16 = (f32[3,4096]{1,0:T(4,128)}, f32[3,4096]{1,0:T(4,128)S(1)}, u32[]{:S(2)}, u32[]{:S(2)}) collective-permute-start(f32[3,4096]{1,0:T(4,128)} %psum.7), channel_id=1, source_target_pairs={{16,0},{17,1},{18,2},{19,3},{20,4},{21,5},{22,6},{23,7},{24,8},{25... | collective-permute-start | bytes 147464 | tf_op jit(solution)/shard_map/ppermute | solution.py:88
  155.1 6.0 %copy-start = (bf16[3,640,256]{2,1,0:T(8,128)(2,1)S(1)}, bf16[3,640,256]{2,1,0:T(8,128)(2,1)}, u32[]{:S(2)}) copy-start(bf16[3,640,256]{2,1,0:T(8,128)(2,1)} %constant_dynamic-update-slice_fusion.9) | copy-start | bytes 2949124
  155.1 9.4 %collective-permute-start = (bf16[3,160,256]{2,1,0:T(8,128)(2,1)S(1)}, bf16[3,160,256]{2,1,0:T(8,128)(2,1)}, u32[]{:S(2)}, u32[]{:S(2)}) collective-permute-start(bf16[3,160,256]{2,1,0:T(8,128)(2,1)S(1)} %get-tuple-element.21), channel_id=1, source_target_pairs={{16,0},{17,1},{18,2},{19,3},{20,4},{21,5},{22,6},{23,7},{24,8},{25... | collective-permute-start | bytes 737288 | tf_op jit(solution)/shard_map/ppermute | solution.py:82
  157.4 34.3 %copy-start.24 = (bf16[3,160,256]{2,1,0:T(8,128)(2,1)S(1)}, bf16[3,160,256]{2,1,0:T(8,128)(2,1)}, u32[]{:S(2)}) copy-start(bf16[3,160,256]{2,1,0:T(8,128)(2,1)} %get-tuple-element.23) | copy-start | bytes 737284
  157.4 10.0 %collective-permute-start.1 = (bf16[3,160,256]{2,1,0:T(8,128)(2,1)}, bf16[3,160,256]{2,1,0:T(8,128)(2,1)}, u32[]{:S(2)}, u32[]{:S(2)}) collective-permute-start(bf16[3,160,256]{2,1,0:T(8,128)(2,1)} %get-tuple-element.25), channel_id=1, source_target_pairs={{16,0},{17,1},{18,2},{19,3},{20,4},{21,5},{22,6},{23,7},{24,8},{25... | collective-permute-start | bytes 737288 | tf_op jit(solution)/shard_map/ppermute | solution.py:82
  159.7 7.7 %copy-start.25 = (bf16[3,160,256]{2,1,0:T(8,128)(2,1)S(1)}, bf16[3,160,256]{2,1,0:T(8,128)(2,1)}, u32[]{:S(2)}) copy-start(bf16[3,160,256]{2,1,0:T(8,128)(2,1)} %get-tuple-element.28) | copy-start | bytes 737284
  159.7 13.0 %collective-permute-start.2 = (bf16[3,160,256]{2,1,0:T(8,128)(2,1)}, bf16[3,160,256]{2,1,0:T(8,128)(2,1)S(1)}, u32[]{:S(2)}, u32[]{:S(2)}) collective-permute-start(bf16[3,160,256]{2,1,0:T(8,128)(2,1)} %get-tuple-element.29), channel_id=1, source_target_pairs={{16,0},{17,1},{18,2},{19,3},{20,4},{21,5},{22,6},{23,7},{24,8},{25... | collective-permute-start | bytes 737288 | tf_op jit(solution)/shard_map/ppermute | solution.py:82
  161.9 16.0 %collective-permute-start.3 = (bf16[3,160,256]{2,1,0:T(8,128)(2,1)}, bf16[3,160,256]{2,1,0:T(8,128)(2,1)S(1)}, u32[]{:S(2)}, u32[]{:S(2)}) collective-permute-start(bf16[3,160,256]{2,1,0:T(8,128)(2,1)} %get-tuple-element.33), channel_id=1, source_target_pairs={{16,0},{17,1},{18,2},{19,3},{20,4},{21,5},{22,6},{23,7},{24,8},{25... | collective-permute-start | bytes 737288 | tf_op jit(solution)/shard_map/ppermute | solution.py:82
  163.2 28.5 %collective-permute-start.4 = (bf16[3,160,256]{2,1,0:T(8,128)(2,1)}, bf16[3,160,256]{2,1,0:T(8,128)(2,1)S(1)}, u32[]{:S(2)}, u32[]{:S(2)}) collective-permute-start(bf16[3,160,256]{2,1,0:T(8,128)(2,1)} %get-tuple-element.20), channel_id=1, source_target_pairs={{16,1},{17,2},{18,3},{19,0},{20,5},{21,6},{22,7},{23,4},{24,9},{25... | collective-permute-start | bytes 737288 | tf_op jit(solution)/shard_map/ppermute | solution.py:82
  164.5 32.4 %collective-permute-start.5 = (bf16[3,160,256]{2,1,0:T(8,128)(2,1)}, bf16[3,160,256]{2,1,0:T(8,128)(2,1)S(1)}, u32[]{:S(2)}, u32[]{:S(2)}) collective-permute-start(bf16[3,160,256]{2,1,0:T(8,128)(2,1)} %get-tuple-element.24), channel_id=1, source_target_pairs={{16,1},{17,2},{18,3},{19,0},{20,5},{21,6},{22,7},{23,4},{24,9},{25... | collective-permute-start | bytes 737288 | tf_op jit(solution)/shard_map/ppermute | solution.py:82
  167.4 34.8 %collective-permute-start.6 = (bf16[3,160,256]{2,1,0:T(8,128)(2,1)S(1)}, bf16[3,160,256]{2,1,0:T(8,128)(2,1)S(1)}, u32[]{:S(2)}, u32[]{:S(2)}) collective-permute-start(bf16[3,160,256]{2,1,0:T(8,128)(2,1)S(1)} %copy-done.25), channel_id=1, source_target_pairs={{16,1},{17,2},{18,3},{19,0},{20,5},{21,6},{22,7},{23,4},{24,9},{25... | collective-permute-start | bytes 737288 | tf_op jit(solution)/shard_map/ppermute | solution.py:82
  172.7 34.5 %collective-permute-start.7 = (bf16[3,160,256]{2,1,0:T(8,128)(2,1)S(1)}, bf16[3,160,256]{2,1,0:T(8,128)(2,1)S(1)}, u32[]{:S(2)}, u32[]{:S(2)}) collective-permute-start(bf16[3,160,256]{2,1,0:T(8,128)(2,1)S(1)} %get-tuple-element.32), channel_id=1, source_target_pairs={{16,1},{17,2},{18,3},{19,0},{20,5},{21,6},{22,7},{23,4},{24,9},{25... | collective-permute-start | bytes 737288 | tf_op jit(solution)/shard_map/ppermute | solution.py:82
  177.8 30.6 %collective-permute-start.8 = (bf16[3,160,256]{2,1,0:T(8,128)(2,1)S(1)}, bf16[3,160,256]{2,1,0:T(8,128)(2,1)S(1)}, u32[]{:S(2)}, u32[]{:S(2)}) collective-permute-start(bf16[3,160,256]{2,1,0:T(8,128)(2,1)S(1)} %get-tuple-element.19), channel_id=1, source_target_pairs={{16,2},{17,3},{18,0},{19,1},{20,6},{21,7},{22,4},{23,5},{24,10},{2... | collective-permute-start | bytes 737288 | tf_op jit(solution)/shard_map/ppermute | solution.py:82
  191.7 22.2 %collective-permute-start.9 = (bf16[3,160,256]{2,1,0:T(8,128)(2,1)S(1)}, bf16[3,160,256]{2,1,0:T(8,128)(2,1)S(1)}, u32[]{:S(2)}, u32[]{:S(2)}) collective-permute-start(bf16[3,160,256]{2,1,0:T(8,128)(2,1)S(1)} %copy-done.24), channel_id=1, source_target_pairs={{16,2},{17,3},{18,0},{19,1},{20,6},{21,7},{22,4},{23,5},{24,10},{2... | collective-permute-start | bytes 737288 | tf_op jit(solution)/shard_map/ppermute | solution.py:82
  196.9 22.2 %collective-permute-start.10 = (bf16[3,160,256]{2,1,0:T(8,128)(2,1)S(1)}, bf16[3,160,256]{2,1,0:T(8,128)(2,1)S(1)}, u32[]{:S(2)}, u32[]{:S(2)}) collective-permute-start(bf16[3,160,256]{2,1,0:T(8,128)(2,1)S(1)} %get-tuple-element.27), channel_id=1, source_target_pairs={{16,2},{17,3},{18,0},{19,1},{20,6},{21,7},{22,4},{23,5},{24,10},{2... | collective-permute-start | bytes 737288 | tf_op jit(solution)/shard_map/ppermute | solution.py:82
  202.2 22.2 %collective-permute-start.11 = (bf16[3,160,256]{2,1,0:T(8,128)(2,1)S(1)}, bf16[3,160,256]{2,1,0:T(8,128)(2,1)S(1)}, u32[]{:S(2)}, u32[]{:S(2)}) collective-permute-start(bf16[3,160,256]{2,1,0:T(8,128)(2,1)S(1)} %get-tuple-element.31), channel_id=1, source_target_pairs={{16,2},{17,3},{18,0},{19,1},{20,6},{21,7},{22,4},{23,5},{24,10},{2... | collective-permute-start | bytes 737288 | tf_op jit(solution)/shard_map/ppermute | solution.py:82
  207.2 30.7 %collective-permute-start.12 = (bf16[3,160,256]{2,1,0:T(8,128)(2,1)S(1)}, bf16[3,160,256]{2,1,0:T(8,128)(2,1)S(1)}, u32[]{:S(2)}, u32[]{:S(2)}) collective-permute-start(bf16[3,160,256]{2,1,0:T(8,128)(2,1)S(1)} %get-tuple-element.18), channel_id=1, source_target_pairs={{16,3},{17,0},{18,1},{19,2},{20,7},{21,4},{22,5},{23,6},{24,11},{2... | collective-permute-start | bytes 737288 | tf_op jit(solution)/shard_map/ppermute | solution.py:82
  208.5 34.7 %collective-permute-start.13 = (bf16[3,160,256]{2,1,0:T(8,128)(2,1)S(1)}, bf16[3,160,256]{2,1,0:T(8,128)(2,1)S(1)}, u32[]{:S(2)}, u32[]{:S(2)}) collective-permute-start(bf16[3,160,256]{2,1,0:T(8,128)(2,1)S(1)} %get-tuple-element.22), channel_id=1, source_target_pairs={{16,3},{17,0},{18,1},{19,2},{20,7},{21,4},{22,5},{23,6},{24,11},{2... | collective-permute-start | bytes 737288 | tf_op jit(solution)/shard_map/ppermute | solution.py:82
  213.8 33.0 %collective-permute-start.14 = (bf16[3,160,256]{2,1,0:T(8,128)(2,1)S(1)}, bf16[3,160,256]{2,1,0:T(8,128)(2,1)S(1)}, u32[]{:S(2)}, u32[]{:S(2)}) collective-permute-start(bf16[3,160,256]{2,1,0:T(8,128)(2,1)S(1)} %get-tuple-element.26), channel_id=1, source_target_pairs={{16,3},{17,0},{18,1},{19,2},{20,7},{21,4},{22,5},{23,6},{24,11},{2... | collective-permute-start | bytes 737288 | tf_op jit(solution)/shard_map/ppermute | solution.py:82
  219.1 30.3 %collective-permute-start.15 = (bf16[3,160,256]{2,1,0:T(8,128)(2,1)S(1)}, bf16[3,160,256]{2,1,0:T(8,128)(2,1)S(1)}, u32[]{:S(2)}, u32[]{:S(2)}) collective-permute-start(bf16[3,160,256]{2,1,0:T(8,128)(2,1)S(1)} %get-tuple-element.30), channel_id=1, source_target_pairs={{16,3},{17,0},{18,1},{19,2},{20,7},{21,4},{22,5},{23,6},{24,11},{2... | collective-permute-start | bytes 737288 | tf_op jit(solution)/shard_map/ppermute | solution.py:82
  249.5 1.9 copy-start.1
where the time goes:
time: 253 us; the launch traced here: 251 us
  waiting for transfers between devices  68.1 us (27%)
  matrix products  55.1 us (22%)
  blocking collectives  53.4 us (21%)
  local copies, waits for them, and re-layouts  47.7 us (19%)
  starting transfers between devices  22.2 us (9%)
  other arithmetic  3.64 us (1%)
    ppermute x16, waiting for transfers between devices, per_device(): arrived[shift][c] = lax.ppermute(piece, ('section', 'mp'), pairs(shift))  68.1 us
    psum x1, blocking collectives, per_device(): totals = lax.psum(slots, ('dp', 'mp'))  53.4 us
    ppermute x16, starting transfers between devices, per_device(): arrived[shift][c] = lax.ppermute(piece, ('section', 'mp'), pairs(shift))  20.9 us
    dot_general x4, matrix products, chunk_grads(): jnp.einsum('bhqk,bkhd->bqhd', grad_scores, k, preferred_element_type=jnp....  15.1 us
    dot_general x4, matrix products, chunk_grads(): jnp.einsum('bhqk,bqhd->bkhd', grad_scores, q, preferred_element_type=jnp....  14.5 us
    another operation x16, local copies, waits for them, and re-layouts, chunk_grads(): blocks = jnp.stack([grad_q, grad_k, grad_v]).astype(jnp.bfloat16)  12.4 us
    dot_general x4, matrix products, chunk_grads(): jnp.einsum('bhqk,bqhd->bkhd', attn_low, g, preferred_element_type=jnp.flo...  11 us
    sub x4, matrix products, chunk_grads(): expont = jnp.exp(scores - highest)  9.71 us
  transfers between devices with their start and end apart: 17, of which 14 were waited for; matrix products, arithmetic and copies ran while one was open for 2% of the time, Pallas kernels for 0%

commit v1 on v0

--- a/solution.py
+++ b/solution.py
@@ -84,7 +84,7 @@
     slots = lax.dynamic_update_slice_in_dim(
         jnp.zeros((3, columns * parts), jnp.float32), own, part * columns, 1
     )
-    totals = lax.psum(slots, ("dp", "mp"))
+    totals = lax.psum(lax.psum(slots, "mp"), "dp")
     totals = lax.ppermute(totals, "section", [(s + 1, s) for s in range(sections - 1)])
     bias_grad = totals / math.sqrt(replicas * length)
     received = jnp.zeros((3, rows, columns * parts), jnp.bfloat16)

time: 253 us -> 224 us (0.89)
  blocking collectives: 53.4 us -> 27.9 us
  waiting for transfers between devices: 68.1 us -> 63.4 us
    psum x1 -> x2, blocking collectives: 53.4 us -> 27.9 us  [per_device(): totals = lax.psum(lax.psum(slots, 'mp'), 'dp')]
    ppermute x16, waiting for transfers between devices: 68.1 us -> 63.4 us  [per_device(): arrived[shift][c] = lax.ppermute(piece, ('section', 'mp'), pairs(shift))]
  transfers between devices with their start and end apart: 17 -> 17, of which waited for: 14 -> 13; matrix products, arithmetic and copies ran while one was open for 2% -> 3% of each run, Pallas kernels for 0% -> 0%
where the time goes in v1:
time: 224 us; the launch traced here: 221 us
  waiting for transfers between devices  63.4 us (28%)
  matrix products  55.1 us (25%)
  local copies, waits for them, and re-layouts  47.7 us (21%)
  blocking collectives  27.9 us (12%)
  starting transfers between devices  22.2 us (10%)
  other arithmetic  3.64 us (2%)
    ppermute x16, waiting for transfers between devices, per_device(): arrived[shift][c] = lax.ppermute(piece, ('section', 'mp'), pairs(shift))  63.4 us
    psum x2, blocking collectives, per_device(): totals = lax.psum(lax.psum(slots, 'mp'), 'dp')  27.9 us
    ppermute x16, starting transfers between devices, per_device(): arrived[shift][c] = lax.ppermute(piece, ('section', 'mp'), pairs(shift))  20.9 us
    dot_general x4, matrix products, chunk_grads(): jnp.einsum('bhqk,bkhd->bqhd', grad_scores, k, preferred_element_type=jnp....  15.1 us
    dot_general x4, matrix products, chunk_grads(): jnp.einsum('bhqk,bqhd->bkhd', grad_scores, q, preferred_element_type=jnp....  14.5 us
    another operation x16, local copies, waits for them, and re-layouts, chunk_grads(): blocks = jnp.stack([grad_q, grad_k, grad_v]).astype(jnp.bfloat16)  12.4 us
    dot_general x4, matrix products, chunk_grads(): jnp.einsum('bhqk,bqhd->bkhd', attn_low, g, preferred_element_type=jnp.flo...  11 us
    sub x4, matrix products, chunk_grads(): expont = jnp.exp(scores - highest)  9.71 us
  transfers between devices with their start and end apart: 17, of which 13 were waited for; matrix products, arithmetic and copies ran while one was open for 3% of the time, Pallas kernels for 0%

profile of v1, /device:TPU:5, one launch (start us, length us, event | category | flops | bytes accessed | tf_op | source)
XLA Modules:
  0.0 221.3 jit_solution(6763914935326599817)
XLA Ops:
  0.7 2.3 %fusion.237 = (bf16[640,256]{1,0:T(8,128)(2,1)S(1)}, bf16[640,256]{1,0:T(8,128)(2,1)S(1)}, bf16[640,256]{1,0:T(8,128)(2,1)}, bf16[640,256]{1,0:T(8,128)(2,1)}) fusion(bf16[640,1024]{1,0:T(8,128)(2,1)} %bitcast.44), kind=kLoop, calls=%fused_computation.198 | loop fusion | bytes 2621440 | tf_op jit(solution)/shard_map/slice | solution.py:71
  5.7 2.2 %fusion.239 = (bf16[640,256]{1,0:T(8,128)(2,1)S(1)}, bf16[640,256]{1,0:T(8,128)(2,1)S(1)}, bf16[640,256]{1,0:T(8,128)(2,1)}, bf16[640,256]{1,0:T(8,128)(2,1)}) fusion(bf16[640,1024]{1,0:T(8,128)(2,1)} %bitcast.46), kind=kLoop, calls=%fused_computation.200 | loop fusion | bytes 2621440 | tf_op jit(solution)/shard_map/slice | solution.py:74
  10.6 1.5 fusion.135
  12.1 3.2 %fusion.256 = (f32[2,2,320]{2,1,0:T(2,128)S(1)}, f32[2,2,320,320]{2,3,1,0:T(8,128)}) fusion(pred[2,320,320]{1,2,0:T(8,128)(4,1)S(1)} %fusion.124, bf16[2,320,2,128]{3,2,1,0:T(2,128)(2,1)} %reshape.143, bf16[2,320,2,128]{3,2,1,0:T(2,128)(2,1)} %reshape.142), kind=kOutput, calls=%fused_computation.205 | convolution fusion | flops 106496320 | bytes 2503680 | tf_op jit(solution)/shard_map/sub | solution.py:24
  15.3 3.8 %fusion.75 = bf16[2,320,2,128]{3,1,2,0:T(8,128)(2,1)} fusion(f32[2,2,320,320]{2,3,1,0:T(8,128)S(1)} %fusion.135, bf16[2,320,2,128]{3,2,1,0:T(2,128)(2,1)} %reshape.143, f32[2,2,320,320]{2,3,1,0:T(8,128)} %get-tuple-element.41, f32[2,2,320]{2,1,0:T(2,128)S(1)} %get-tuple-element.40), kind=kOutput, calls=%fused_computation.57 | convolution fusion | flops 107890240 | bytes 3937280 | tf_op jit(solution)/shard_map/bhqk,bkhd->bqhd/dot_general | solution.py:31
  19.0 3.6 %fusion.72 = bf16[2,320,2,128]{3,1,2,0:T(8,128)(2,1)} fusion(f32[2,2,320,320]{2,3,1,0:T(8,128)S(1)} %fusion.135, bf16[2,320,2,128]{3,2,1,0:T(2,128)(2,1)} %reshape.142, f32[2,2,320,320]{2,3,1,0:T(8,128)} %get-tuple-element.41, f32[2,2,320]{2,1,0:T(2,128)S(1)} %get-tuple-element.40), kind=kOutput, calls=%fused_computation.56 | convolution fusion | flops 107890240 | bytes 3937280 | tf_op jit(solution)/shard_map/bhqk,bqhd->bkhd/dot_general | solution.py:32
  22.7 2.8 %fusion.96 = bf16[2,320,2,128]{3,1,2,0:T(8,128)(2,1)} fusion(bf16[2,320,2,128]{3,2,1,0:T(2,128)(2,1)} %reshape.144, f32[2,2,320,320]{2,3,1,0:T(8,128)} %get-tuple-element.41, f32[2,2,320]{2,1,0:T(2,128)S(1)} %get-tuple-element.40), kind=kOutput, calls=%fused_computation.64 | convolution fusion | flops 105840640 | bytes 2298880 | tf_op jit(solution)/shard_map/bhqk,bqhd->bkhd/dot_general | solution.py:27
  27.3 2.1 fusion.251
  29.4 1.5 fusion.133
  30.9 3.8 %fusion.81 = bf16[2,320,2,128]{3,1,2,0:T(8,128)(2,1)} fusion(f32[2,2,320,320]{2,3,1,0:T(8,128)S(1)} %fusion.133, bf16[2,320,2,128]{3,2,1,0:T(2,128)(2,1)} %copy-done.22, f32[2,2,320,320]{2,3,1,0:T(8,128)} %get-tuple-element.39, f32[2,2,320]{2,1,0:T(2,128)S(1)} %get-tuple-element.38), kind=kOutput, calls=%fused_computation.59 | convolution fusion | flops 107890240 | bytes 3937280 | tf_op jit(solution)/shard_map/bhqk,bkhd->bqhd/dot_general | solution.py:31
  34.7 3.6 %fusion.78 = bf16[2,320,2,128]{3,1,2,0:T(8,128)(2,1)} fusion(f32[2,2,320,320]{2,3,1,0:T(8,128)S(1)} %fusion.133, bf16[2,320,2,128]{3,2,1,0:T(2,128)(2,1)} %copy-done.20, f32[2,2,320,320]{2,3,1,0:T(8,128)} %get-tuple-element.39, f32[2,2,320]{2,1,0:T(2,128)S(1)} %get-tuple-element.38), kind=kOutput, calls=%fused_computation.58 | convolution fusion | flops 107890240 | bytes 3937280 | tf_op jit(solution)/shard_map/bhqk,bqhd->bkhd/dot_general | solution.py:32
  38.3 2.8 %fusion.97 = bf16[2,320,2,128]{3,1,2,0:T(8,128)(2,1)} fusion(bf16[2,320,2,128]{3,2,1,0:T(2,128)(2,1)} %reshape.148, f32[2,2,320,320]{2,3,1,0:T(8,128)} %get-tuple-element.39, f32[2,2,320]{2,1,0:T(2,128)S(1)} %get-tuple-element.38), kind=kOutput, calls=%fused_computation.65 | convolution fusion | flops 105840640 | bytes 2298880 | tf_op jit(solution)/shard_map/bhqk,bqhd->bkhd/dot_general | solution.py:27
  43.0 2.1 fusion.246
  45.1 1.5 fusion.131
  46.6 3.8 %fusion.87 = bf16[2,320,2,128]{3,1,2,0:T(8,128)(2,1)} fusion(f32[2,2,320,320]{2,3,1,0:T(8,128)S(1)} %fusion.131, bf16[2,320,2,128]{3,2,1,0:T(2,128)(2,1)} %copy-done.23, f32[2,2,320,320]{2,3,1,0:T(8,128)} %get-tuple-element.37, f32[2,2,320]{2,1,0:T(2,128)S(1)} %get-tuple-element.36), kind=kOutput, calls=%fused_computation.61 | convolution fusion | flops 107890240 | bytes 3937280 | tf_op jit(solution)/shard_map/bhqk,bkhd->bqhd/dot_general | solution.py:31
  50.4 3.6 %fusion.84 = bf16[2,320,2,128]{3,1,2,0:T(8,128)(2,1)} fusion(f32[2,2,320,320]{2,3,1,0:T(8,128)S(1)} %fusion.131, bf16[2,320,2,128]{3,2,1,0:T(2,128)(2,1)} %copy-done.21, f32[2,2,320,320]{2,3,1,0:T(8,128)} %get-tuple-element.37, f32[2,2,320]{2,1,0:T(2,128)S(1)} %get-tuple-element.36), kind=kOutput, calls=%fused_computation.60 | convolution fusion | flops 107890240 | bytes 3937280 | tf_op jit(solution)/shard_map/bhqk,bqhd->bkhd/dot_general | solution.py:32
  54.0 2.7 %fusion.98 = bf16[2,320,2,128]{3,1,2,0:T(8,128)(2,1)} fusion(bf16[2,320,2,128]{3,2,1,0:T(2,128)(2,1)} %reshape.152, f32[2,2,320,320]{2,3,1,0:T(8,128)} %get-tuple-element.37, f32[2,2,320]{2,1,0:T(2,128)S(1)} %get-tuple-element.36), kind=kOutput, calls=%fused_computation.66 | convolution fusion | flops 105840640 | bytes 2298880 | tf_op jit(solution)/shard_map/bhqk,bqhd->bkhd/dot_general | solution.py:27
  57.0 2.3 %fusion.241 = (f32[2,2,320]{2,1,0:T(2,128)S(1)}, f32[2,2,320,320]{2,3,1,0:T(8,128)}) fusion(pred[2,320,320]{1,2,0:T(8,128)(4,1)S(1)} %fusion.124, bf16[2,320,2,128]{3,2,1,0:T(2,128)(2,1)S(1)} %reshape.155, bf16[2,320,2,128]{3,2,1,0:T(2,128)(2,1)S(1)} %reshape.154), kind=kOutput, calls=%fused_computation.202 | convolution fusion | flops 106496320 | bytes 2503680 | tf_op jit(solution)/shard_map/sub | solution.py:24
  59.8 3.6 %fusion.90 = bf16[2,320,2,128]{3,1,2,0:T(8,128)(2,1)} fusion(f32[2,2,320,320]{2,3,1,0:T(8,128)S(1)} %fusion.129, bf16[2,320,2,128]{3,2,1,0:T(2,128)(2,1)S(1)} %reshape.154, f32[2,2,320,320]{2,3,1,0:T(8,128)} %get-tuple-element.35, f32[2,2,320]{2,1,0:T(2,128)S(1)} %get-tuple-element.34), kind=kOutput, calls=%fused_computation.62 | convolution fusion | flops 107890240 | bytes 3937280 | tf_op jit(solution)/shard_map/bhqk,bqhd->bkhd/dot_general | solution.py:32
  63.4 3.7 %fusion.93 = bf16[2,320,2,128]{3,1,2,0:T(8,128)(2,1)} fusion(f32[2,2,320,320]{2,3,1,0:T(8,128)S(1)} %fusion.129, bf16[2,320,2,128]{3,2,1,0:T(2,128)(2,1)S(1)} %reshape.155, f32[2,2,320,320]{2,3,1,0:T(8,128)} %get-tuple-element.35, f32[2,2,320]{2,1,0:T(2,128)S(1)} %get-tuple-element.34), kind=kOutput, calls=%fused_computation.63 | convolution fusion | flops 107890240 | bytes 3937280 | tf_op jit(solution)/shard_map/bhqk,bkhd->bqhd/dot_general | solution.py:31
  67.1 2.7 %fusion.99 = bf16[2,320,2,128]{3,1,2,0:T(8,128)(2,1)} fusion(bf16[2,320,2,128]{3,2,1,0:T(2,128)(2,1)S(1)} %reshape.156, f32[2,2,320,320]{2,3,1,0:T(8,128)} %get-tuple-element.35, f32[2,2,320]{2,1,0:T(2,128)S(1)} %get-tuple-element.34), kind=kOutput, calls=%fused_computation.67 | convolution fusion | flops 105840640 | bytes 2298880 | tf_op jit(solution)/shard_map/bhqk,bqhd->bkhd/dot_general | solution.py:27
  75.5 2.0 copy.41
  78.7 2.0 copy.43
  80.7 1.9 stack.58
  86.1 2.0 copy.50
  88.2 1.9 stack.60
  90.1 1.7 constant_dynamic-update-slice_fusion.11
  91.8 2.0 copy.54
  93.8 1.9 stack.62
  96.4 1.7 constant_dynamic-update-slice_fusion.9
  99.6 11.0 %psum.14 = f32[3,4096]{1,0:T(4,128)S(1)} all-reduce(f32[3,4096]{1,0:T(4,128)S(1)} %maximum_dynamic-update-slice_fusion), channel_id=1, replica_groups=mesh['section'=2,'dp'=4,'mp'=4] {'mp'}, use_global_device_ids=true, to_apply=%region_16.17 | all-reduce | flops 12288 | bytes 98304 | tf_op jit(solution)/shard_map/psum | solution.py:87
  110.6 16.8 %psum.15 = f32[3,4096]{1,0:T(4,128)} all-reduce(f32[3,4096]{1,0:T(4,128)S(1)} %psum.14), channel_id=1, replica_groups=mesh['section'=2,'dp'=4,'mp'=4] {'dp'}, use_global_device_ids=true, to_apply=%region_17.18 | all-reduce | flops 12288 | bytes 98304 | tf_op jit(solution)/shard_map/psum | solution.py:87
  129.6 1.4 collective-permute-start
  131.9 1.4 collective-permute-start.1
  134.2 1.4 collective-permute-start.2
  143.0 4.0 %collective-permute-done.2 = bf16[3,160,256]{2,1,0:T(8,128)(2,1)S(1)} collective-permute-done((bf16[3,160,256]{2,1,0:T(8,128)(2,1)}, bf16[3,160,256]{2,1,0:T(8,128)(2,1)S(1)}, u32[]{:S(2)}, u32[]{:S(2)}) %collective-permute-start.2) | collective-permute-done | bytes 245792 | tf_op jit(solution)/shard_map/ppermute | solution.py:82
  148.2 3.9 %collective-permute-done.3 = bf16[3,160,256]{2,1,0:T(8,128)(2,1)S(1)} collective-permute-done((bf16[3,160,256]{2,1,0:T(8,128)(2,1)}, bf16[3,160,256]{2,1,0:T(8,128)(2,1)S(1)}, u32[]{:S(2)}, u32[]{:S(2)}) %collective-permute-start.3) | collective-permute-done | bytes 245792 | tf_op jit(solution)/shard_map/ppermute | solution.py:82
  153.4 11.8 %collective-permute-done.4 = bf16[3,160,256]{2,1,0:T(8,128)(2,1)S(1)} collective-permute-done((bf16[3,160,256]{2,1,0:T(8,128)(2,1)}, bf16[3,160,256]{2,1,0:T(8,128)(2,1)S(1)}, u32[]{:S(2)}, u32[]{:S(2)}) %collective-permute-start.4) | collective-permute-done | bytes 245792 | tf_op jit(solution)/shard_map/ppermute | solution.py:82
  166.5 4.0 %collective-permute-done.5 = bf16[3,160,256]{2,1,0:T(8,128)(2,1)S(1)} collective-permute-done((bf16[3,160,256]{2,1,0:T(8,128)(2,1)}, bf16[3,160,256]{2,1,0:T(8,128)(2,1)S(1)}, u32[]{:S(2)}, u32[]{:S(2)}) %collective-permute-start.5) | collective-permute-done | bytes 245792 | tf_op jit(solution)/shard_map/ppermute | solution.py:82
  172.5 3.0 %collective-permute-done.6 = bf16[3,160,256]{2,1,0:T(8,128)(2,1)S(1)} collective-permute-done((bf16[3,160,256]{2,1,0:T(8,128)(2,1)S(1)}, bf16[3,160,256]{2,1,0:T(8,128)(2,1)S(1)}, u32[]{:S(2)}, u32[]{:S(2)}) %collective-permute-start.6) | collective-permute-done | bytes 245792 | tf_op jit(solution)/shard_map/ppermute | solution.py:82
  178.4 2.3 %collective-permute-done.7 = bf16[3,160,256]{2,1,0:T(8,128)(2,1)S(1)} collective-permute-done((bf16[3,160,256]{2,1,0:T(8,128)(2,1)S(1)}, bf16[3,160,256]{2,1,0:T(8,128)(2,1)S(1)}, u32[]{:S(2)}, u32[]{:S(2)}) %collective-permute-start.7) | collective-permute-done | bytes 245792 | tf_op jit(solution)/shard_map/ppermute | solution.py:82
  184.7 3.8 %collective-permute-done.10 = bf16[3,160,256]{2,1,0:T(8,128)(2,1)S(1)} collective-permute-done((bf16[3,160,256]{2,1,0:T(8,128)(2,1)S(1)}, bf16[3,160,256]{2,1,0:T(8,128)(2,1)S(1)}, u32[]{:S(2)}, u32[]{:S(2)}) %collective-permute-start.10) | collective-permute-done | bytes 245792 | tf_op jit(solution)/shard_map/ppermute | solution.py:82
  189.9 3.9 %collective-permute-done.11 = bf16[3,160,256]{2,1,0:T(8,128)(2,1)S(1)} collective-permute-done((bf16[3,160,256]{2,1,0:T(8,128)(2,1)S(1)}, bf16[3,160,256]{2,1,0:T(8,128)(2,1)S(1)}, u32[]{:S(2)}, u32[]{:S(2)}) %collective-permute-start.11) | collective-permute-done | bytes 245792 | tf_op jit(solution)/shard_map/ppermute | solution.py:82
  193.9 14.3 %collective-permute-done.12 = bf16[3,160,256]{2,1,0:T(8,128)(2,1)S(1)} collective-permute-done((bf16[3,160,256]{2,1,0:T(8,128)(2,1)S(1)}, bf16[3,160,256]{2,1,0:T(8,128)(2,1)S(1)}, u32[]{:S(2)}, u32[]{:S(2)}) %collective-permute-start.12) | collective-permute-done | bytes 245792 | tf_op jit(solution)/shard_map/ppermute | solution.py:82
  208.2 5.3 %collective-permute-done.13 = bf16[3,160,256]{2,1,0:T(8,128)(2,1)S(1)} collective-permute-done((bf16[3,160,256]{2,1,0:T(8,128)(2,1)S(1)}, bf16[3,160,256]{2,1,0:T(8,128)(2,1)S(1)}, u32[]{:S(2)}, u32[]{:S(2)}) %collective-permute-start.13) | collective-permute-done | bytes 245792 | tf_op jit(solution)/shard_map/ppermute | solution.py:82
  213.4 3.2 %collective-permute-done.14 = bf16[3,160,256]{2,1,0:T(8,128)(2,1)S(1)} collective-permute-done((bf16[3,160,256]{2,1,0:T(8,128)(2,1)S(1)}, bf16[3,160,256]{2,1,0:T(8,128)(2,1)S(1)}, u32[]{:S(2)}, u32[]{:S(2)}) %collective-permute-start.14) | collective-permute-done | bytes 245792 | tf_op jit(solution)/shard_map/ppermute | solution.py:82
  216.6 2.6 %collective-permute-done.15 = bf16[3,160,256]{2,1,0:T(8,128)(2,1)S(1)} collective-permute-done((bf16[3,160,256]{2,1,0:T(8,128)(2,1)S(1)}, bf16[3,160,256]{2,1,0:T(8,128)(2,1)S(1)}, u32[]{:S(2)}, u32[]{:S(2)}) %collective-permute-start.15) | collective-permute-done | bytes 245792 | tf_op jit(solution)/shard_map/ppermute | solution.py:82
  219.4 1.9 copy-done.1
  (140 shorter events, 47.3 us)
Async XLA Ops:
  0.6 3.2 %copy-start.10 = (bf16[1,1,640,1024]{3,2,1,0:T(8,128)(2,1)S(1)}, bf16[1,1,640,1024]{3,2,1,0:T(8,128)(2,1)}, u32[]{:S(2)}) copy-start(bf16[1,1,640,1024]{3,2,1,0:T(8,128)(2,1)} %param.6) | copy-start | bytes 3932164
  3.0 2.5 %copy-start.26 = (s32[1,1,640]{2,1,0:T(1,128)S(1)}, s32[1,1,640]{2,1,0:T(1,128)}, u32[]{:S(2)}) copy-start(s32[1,1,640]{2,1,0:T(1,128)} %param.9) | copy-start | bytes 7684
  4.8 3.9 %copy-start.11 = (bf16[1,1,640,1024]{3,2,1,0:T(8,128)(2,1)S(1)}, bf16[1,1,640,1024]{3,2,1,0:T(8,128)(2,1)}, u32[]{:S(2)}) copy-start(bf16[1,1,640,1024]{3,2,1,0:T(8,128)(2,1)} %param.7) | copy-start | bytes 3932164
  22.7 2.8 %copy-start.6 = (bf16[640,256]{1,0:T(8,128)(2,1)S(1)}, bf16[640,256]{1,0:T(8,128)(2,1)}, u32[]{:S(2)}) copy-start(bf16[640,256]{1,0:T(8,128)(2,1)} %get-tuple-element.5) | copy-start | bytes 983044
  22.7 2.9 %copy-start.7 = (bf16[640,256]{1,0:T(8,128)(2,1)S(1)}, bf16[640,256]{1,0:T(8,128)(2,1)}, u32[]{:S(2)}) copy-start(bf16[640,256]{1,0:T(8,128)(2,1)} %get-tuple-element.9) | copy-start | bytes 983044
  22.7 3.0 %copy-start.8 = (bf16[640,256]{1,0:T(8,128)(2,1)S(1)}, bf16[640,256]{1,0:T(8,128)(2,1)}, u32[]{:S(2)}) copy-start(bf16[640,256]{1,0:T(8,128)(2,1)} %get-tuple-element.13) | copy-start | bytes 983044
  25.5 1.0 copy-start.9
  25.5 1.7 copy-start.20
  25.7 1.6 copy-start.22
  38.3 2.8 %copy-start.2 = (bf16[640,256]{1,0:T(8,128)(2,1)S(1)}, bf16[640,256]{1,0:T(8,128)(2,1)}, u32[]{:S(2)}) copy-start(bf16[640,256]{1,0:T(8,128)(2,1)} %get-tuple-element.4) | copy-start | bytes 983044
  38.3 2.9 %copy-start.3 = (bf16[640,256]{1,0:T(8,128)(2,1)S(1)}, bf16[640,256]{1,0:T(8,128)(2,1)}, u32[]{:S(2)}) copy-start(bf16[640,256]{1,0:T(8,128)(2,1)} %get-tuple-element.8) | copy-start | bytes 983044
  38.3 3.0 %copy-start.4 = (bf16[640,256]{1,0:T(8,128)(2,1)S(1)}, bf16[640,256]{1,0:T(8,128)(2,1)}, u32[]{:S(2)}) copy-start(bf16[640,256]{1,0:T(8,128)(2,1)} %get-tuple-element.12) | copy-start | bytes 983044
  41.1 1.0 copy-start.5
  41.2 1.8 copy-start.21
  41.3 1.7 copy-start.23
  67.1 2.7 %copy-start.16 = (bf16[2,320,2,128]{3,1,2,0:T(8,128)(2,1)S(1)}, bf16[2,320,2,128]{3,1,2,0:T(8,128)(2,1)}, u32[]{:S(2)}) copy-start(bf16[2,320,2,128]{3,1,2,0:T(8,128)(2,1)} %fusion.75) | copy-start | bytes 983044
  69.8 1.0 copy-start.13
  69.8 1.5 copy-start.12
  71.4 1.0 copy-start.17
  72.0 1.0 copy-start.15
  72.0 1.5 copy-start.14
  73.9 1.0 copy-start.18
  82.6 1.2 copy-start.19
  127.4 10.2 %collective-permute-start.16 = (f32[3,4096]{1,0:T(4,128)}, f32[3,4096]{1,0:T(4,128)S(1)}, u32[]{:S(2)}, u32[]{:S(2)}) collective-permute-start(f32[3,4096]{1,0:T(4,128)} %psum.15), channel_id=1, source_target_pairs={{16,0},{17,1},{18,2},{19,3},{20,4},{21,5},{22,6},{23,7},{24,8},{25... | collective-permute-start | bytes 147464 | tf_op jit(solution)/shard_map/ppermute | solution.py:88
  129.6 6.0 %copy-start = (bf16[3,640,256]{2,1,0:T(8,128)(2,1)S(1)}, bf16[3,640,256]{2,1,0:T(8,128)(2,1)}, u32[]{:S(2)}) copy-start(bf16[3,640,256]{2,1,0:T(8,128)(2,1)} %constant_dynamic-update-slice_fusion.9) | copy-start | bytes 2949124
  129.6 9.4 %collective-permute-start = (bf16[3,160,256]{2,1,0:T(8,128)(2,1)S(1)}, bf16[3,160,256]{2,1,0:T(8,128)(2,1)}, u32[]{:S(2)}, u32[]{:S(2)}) collective-permute-start(bf16[3,160,256]{2,1,0:T(8,128)(2,1)S(1)} %get-tuple-element.21), channel_id=1, source_target_pairs={{16,0},{17,1},{18,2},{19,3},{20,4},{21,5},{22,6},{23,7},{24,8},{25... | collective-permute-start | bytes 737288 | tf_op jit(solution)/shard_map/ppermute | solution.py:82
  131.9 33.4 %copy-start.24 = (bf16[3,160,256]{2,1,0:T(8,128)(2,1)S(1)}, bf16[3,160,256]{2,1,0:T(8,128)(2,1)}, u32[]{:S(2)}) copy-start(bf16[3,160,256]{2,1,0:T(8,128)(2,1)} %get-tuple-element.23) | copy-start | bytes 737284
  131.9 9.8 %collective-permute-start.1 = (bf16[3,160,256]{2,1,0:T(8,128)(2,1)}, bf16[3,160,256]{2,1,0:T(8,128)(2,1)}, u32[]{:S(2)}, u32[]{:S(2)}) collective-permute-start(bf16[3,160,256]{2,1,0:T(8,128)(2,1)} %get-tuple-element.25), channel_id=1, source_target_pairs={{16,0},{17,1},{18,2},{19,3},{20,4},{21,5},{22,6},{23,7},{24,8},{25... | collective-permute-start | bytes 737288 | tf_op jit(solution)/shard_map/ppermute | solution.py:82
  134.2 7.5 %copy-start.25 = (bf16[3,160,256]{2,1,0:T(8,128)(2,1)S(1)}, bf16[3,160,256]{2,1,0:T(8,128)(2,1)}, u32[]{:S(2)}) copy-start(bf16[3,160,256]{2,1,0:T(8,128)(2,1)} %get-tuple-element.28) | copy-start | bytes 737284
  134.2 12.8 %collective-permute-start.2 = (bf16[3,160,256]{2,1,0:T(8,128)(2,1)}, bf16[3,160,256]{2,1,0:T(8,128)(2,1)S(1)}, u32[]{:S(2)}, u32[]{:S(2)}) collective-permute-start(bf16[3,160,256]{2,1,0:T(8,128)(2,1)} %get-tuple-element.29), channel_id=1, source_target_pairs={{16,0},{17,1},{18,2},{19,3},{20,4},{21,5},{22,6},{23,7},{24,8},{25... | collective-permute-start | bytes 737288 | tf_op jit(solution)/shard_map/ppermute | solution.py:82
  136.4 15.7 %collective-permute-start.3 = (bf16[3,160,256]{2,1,0:T(8,128)(2,1)}, bf16[3,160,256]{2,1,0:T(8,128)(2,1)S(1)}, u32[]{:S(2)}, u32[]{:S(2)}) collective-permute-start(bf16[3,160,256]{2,1,0:T(8,128)(2,1)} %get-tuple-element.33), channel_id=1, source_target_pairs={{16,0},{17,1},{18,2},{19,3},{20,4},{21,5},{22,6},{23,7},{24,8},{25... | collective-permute-start | bytes 737288 | tf_op jit(solution)/shard_map/ppermute | solution.py:82
  137.7 27.6 %collective-permute-start.4 = (bf16[3,160,256]{2,1,0:T(8,128)(2,1)}, bf16[3,160,256]{2,1,0:T(8,128)(2,1)S(1)}, u32[]{:S(2)}, u32[]{:S(2)}) collective-permute-start(bf16[3,160,256]{2,1,0:T(8,128)(2,1)} %get-tuple-element.20), channel_id=1, source_target_pairs={{16,1},{17,2},{18,3},{19,0},{20,5},{21,6},{22,7},{23,4},{24,9},{25... | collective-permute-start | bytes 737288 | tf_op jit(solution)/shard_map/ppermute | solution.py:82
  139.0 31.5 %collective-permute-start.5 = (bf16[3,160,256]{2,1,0:T(8,128)(2,1)}, bf16[3,160,256]{2,1,0:T(8,128)(2,1)S(1)}, u32[]{:S(2)}, u32[]{:S(2)}) collective-permute-start(bf16[3,160,256]{2,1,0:T(8,128)(2,1)} %get-tuple-element.24), channel_id=1, source_target_pairs={{16,1},{17,2},{18,3},{19,0},{20,5},{21,6},{22,7},{23,4},{24,9},{25... | collective-permute-start | bytes 737288 | tf_op jit(solution)/shard_map/ppermute | solution.py:82
  141.7 33.8 %collective-permute-start.6 = (bf16[3,160,256]{2,1,0:T(8,128)(2,1)S(1)}, bf16[3,160,256]{2,1,0:T(8,128)(2,1)S(1)}, u32[]{:S(2)}, u32[]{:S(2)}) collective-permute-start(bf16[3,160,256]{2,1,0:T(8,128)(2,1)S(1)} %copy-done.25), channel_id=1, source_target_pairs={{16,1},{17,2},{18,3},{19,0},{20,5},{21,6},{22,7},{23,4},{24,9},{25... | collective-permute-start | bytes 737288 | tf_op jit(solution)/shard_map/ppermute | solution.py:82
  146.9 33.8 %collective-permute-start.7 = (bf16[3,160,256]{2,1,0:T(8,128)(2,1)S(1)}, bf16[3,160,256]{2,1,0:T(8,128)(2,1)S(1)}, u32[]{:S(2)}, u32[]{:S(2)}) collective-permute-start(bf16[3,160,256]{2,1,0:T(8,128)(2,1)S(1)} %get-tuple-element.32), channel_id=1, source_target_pairs={{16,1},{17,2},{18,3},{19,0},{20,5},{21,6},{22,7},{23,4},{24,9},{25... | collective-permute-start | bytes 737288 | tf_op jit(solution)/shard_map/ppermute | solution.py:82
  152.1 29.9 %collective-permute-start.8 = (bf16[3,160,256]{2,1,0:T(8,128)(2,1)S(1)}, bf16[3,160,256]{2,1,0:T(8,128)(2,1)S(1)}, u32[]{:S(2)}, u32[]{:S(2)}) collective-permute-start(bf16[3,160,256]{2,1,0:T(8,128)(2,1)S(1)} %get-tuple-element.19), channel_id=1, source_target_pairs={{16,2},{17,3},{18,0},{19,1},{20,6},{21,7},{22,4},{23,5},{24,10},{2... | collective-permute-start | bytes 737288 | tf_op jit(solution)/shard_map/ppermute | solution.py:82
  165.2 18.1 %collective-permute-start.9 = (bf16[3,160,256]{2,1,0:T(8,128)(2,1)S(1)}, bf16[3,160,256]{2,1,0:T(8,128)(2,1)S(1)}, u32[]{:S(2)}, u32[]{:S(2)}) collective-permute-start(bf16[3,160,256]{2,1,0:T(8,128)(2,1)S(1)} %copy-done.24), channel_id=1, source_target_pairs={{16,2},{17,3},{18,0},{19,1},{20,6},{21,7},{22,4},{23,5},{24,10},{2... | collective-permute-start | bytes 737288 | tf_op jit(solution)/shard_map/ppermute | solution.py:82
  170.5 18.0 %collective-permute-start.10 = (bf16[3,160,256]{2,1,0:T(8,128)(2,1)S(1)}, bf16[3,160,256]{2,1,0:T(8,128)(2,1)S(1)}, u32[]{:S(2)}, u32[]{:S(2)}) collective-permute-start(bf16[3,160,256]{2,1,0:T(8,128)(2,1)S(1)} %get-tuple-element.27), channel_id=1, source_target_pairs={{16,2},{17,3},{18,0},{19,1},{20,6},{21,7},{22,4},{23,5},{24,10},{2... | collective-permute-start | bytes 737288 | tf_op jit(solution)/shard_map/ppermute | solution.py:82
  175.5 18.3 %collective-permute-start.11 = (bf16[3,160,256]{2,1,0:T(8,128)(2,1)S(1)}, bf16[3,160,256]{2,1,0:T(8,128)(2,1)S(1)}, u32[]{:S(2)}, u32[]{:S(2)}) collective-permute-start(bf16[3,160,256]{2,1,0:T(8,128)(2,1)S(1)} %get-tuple-element.31), channel_id=1, source_target_pairs={{16,2},{17,3},{18,0},{19,1},{20,6},{21,7},{22,4},{23,5},{24,10},{2... | collective-permute-start | bytes 737288 | tf_op jit(solution)/shard_map/ppermute | solution.py:82
  180.8 27.4 %collective-permute-start.12 = (bf16[3,160,256]{2,1,0:T(8,128)(2,1)S(1)}, bf16[3,160,256]{2,1,0:T(8,128)(2,1)S(1)}, u32[]{:S(2)}, u32[]{:S(2)}) collective-permute-start(bf16[3,160,256]{2,1,0:T(8,128)(2,1)S(1)} %get-tuple-element.18), channel_id=1, source_target_pairs={{16,3},{17,0},{18,1},{19,2},{20,7},{21,4},{22,5},{23,6},{24,11},{2... | collective-permute-start | bytes 737288 | tf_op jit(solution)/shard_map/ppermute | solution.py:82
  182.1 31.4 %collective-permute-start.13 = (bf16[3,160,256]{2,1,0:T(8,128)(2,1)S(1)}, bf16[3,160,256]{2,1,0:T(8,128)(2,1)S(1)}, u32[]{:S(2)}, u32[]{:S(2)}) collective-permute-start(bf16[3,160,256]{2,1,0:T(8,128)(2,1)S(1)} %get-tuple-element.22), channel_id=1, source_target_pairs={{16,3},{17,0},{18,1},{19,2},{20,7},{21,4},{22,5},{23,6},{24,11},{2... | collective-permute-start | bytes 737288 | tf_op jit(solution)/shard_map/ppermute | solution.py:82
  183.4 33.2 %collective-permute-start.14 = (bf16[3,160,256]{2,1,0:T(8,128)(2,1)S(1)}, bf16[3,160,256]{2,1,0:T(8,128)(2,1)S(1)}, u32[]{:S(2)}, u32[]{:S(2)}) collective-permute-start(bf16[3,160,256]{2,1,0:T(8,128)(2,1)S(1)} %get-tuple-element.26), channel_id=1, source_target_pairs={{16,3},{17,0},{18,1},{19,2},{20,7},{21,4},{22,5},{23,6},{24,11},{2... | collective-permute-start | bytes 737288 | tf_op jit(solution)/shard_map/ppermute | solution.py:82
  188.5 30.8 %collective-permute-start.15 = (bf16[3,160,256]{2,1,0:T(8,128)(2,1)S(1)}, bf16[3,160,256]{2,1,0:T(8,128)(2,1)S(1)}, u32[]{:S(2)}, u32[]{:S(2)}) collective-permute-start(bf16[3,160,256]{2,1,0:T(8,128)(2,1)S(1)} %get-tuple-element.30), channel_id=1, source_target_pairs={{16,3},{17,0},{18,1},{19,2},{20,7},{21,4},{22,5},{23,6},{24,11},{2... | collective-permute-start | bytes 737288 | tf_op jit(solution)/shard_map/ppermute | solution.py:82
  219.4 1.9 copy-start.1
